TPU v7x, 512 devices: a whole 4x8x8 slice. The times are simulated.
512 devices in a mesh: param: 32 (over x, z), ex: 16 (over y, core).
Axes of the slice: x: 4, y: 8, z: 8, core: 2. Of those that a mesh axis runs over, the one named last changes fastest.
Arguments:
- adapter_gradients: bfloat16 [512, 131072], P('ex', 'param'), may hold values from -560 to 560
- sign_hash_keys: int32 [4], replicated, may hold values from 1 to 16777215
- target_indices: int32 [256], replicated, may hold values from 0 to 511
Outputs:
- features: float32 [512, 8192], P('ex', 'param')
- scores: float32 [512, 256], P('ex')
All inputs are finite; a program needn't handle non-finite values.
Results may differ from a plain program's by a relative error of at most 0.0003.
Values sent between devices are 32-bit elements; how exact they have to be, the bound alone decides.
No kernel may reach another device: no remote copies, remote signals or barrier semaphores. Data moves between devices by JAX's collectives and lax.ppermute only.
A program may use at most 128 MiB of HBM per device.

v0:
```python
import jax
import jax.numpy as jnp
from jax import lax
from jax.sharding import PartitionSpec as P

K = 8192
norm_eps = 1e-06


def sign_block(sign_hash_keys, first_row, row_count, col_count):
    mult_row = sign_hash_keys[0] | 1
    mult_col = sign_hash_keys[1] | 1
    seed_add = sign_hash_keys[2]
    mix_mult = sign_hash_keys[3] | 1
    row_ids = first_row + lax.iota(jnp.int32, row_count)[:, None]
    col_ids = lax.iota(jnp.int32, col_count)[None, :]
    hashed = row_ids * mult_row + col_ids * mult_col + seed_add
    hashed = hashed ^ lax.shift_right_logical(hashed, jnp.full_like(hashed, 16))
    hashed = hashed * mix_mult
    hashed = hashed ^ lax.shift_right_logical(hashed, jnp.full_like(hashed, 13))
    hashed = hashed * jnp.int32(-1028477387)
    hashed = hashed ^ lax.shift_right_logical(hashed, jnp.full_like(hashed, 16))
    return jnp.where(hashed < 0, 1.0, -1.0).astype(jnp.bfloat16)


def local(adapter_gradients, sign_hash_keys, target_indices):
    resident_example, resident_rows = adapter_gradients.shape
    row_base = lax.axis_index("param") * jnp.int32(resident_rows)
    turn_count = 8
    rows_per_tile = resident_rows // turn_count
    scale_k = jnp.float32(K)

    def accumulate(tile_idx, totals):
        start_offset = tile_idx * jnp.int32(rows_per_tile)
        gradient_slab = lax.dynamic_slice_in_dim(adapter_gradients, start_offset, rows_per_tile, 1)
        signs = sign_block(sign_hash_keys, row_base + start_offset, rows_per_tile, K)
        return totals + jnp.dot(gradient_slab, signs, preferred_element_type=jnp.float32)

    partial_sums = lax.fori_loop(
        jnp.int32(0),
        jnp.int32(turn_count),
        accumulate,
        jnp.zeros((resident_example, K), jnp.float32),
    )
    projected = lax.psum_scatter(partial_sums, "param", scatter_dimension=1, tiled=True)
    own_squares = jnp.sum(projected * projected, axis=1)
    total_sq = lax.psum(own_squares, "param")
    features = projected * jnp.sqrt(scale_k / (total_sq + norm_eps))[:, None]
    pool_rows = lax.all_gather(features, "ex", axis=0, tiled=True)
    targets = jnp.take(pool_rows, target_indices, axis=0)
    partial_dots = jnp.dot(features, targets.T, precision=lax.Precision.HIGHEST)
    scores = lax.psum(partial_dots, "param") / scale_k
    return (features, scores)


def solution(mesh):
    return jax.shard_map(
        local,
        mesh=mesh,
        in_specs=(P("ex", "param"), P(), P()),
        out_specs=(P("ex", "param"), P("ex", None)),
        check_vma=False,
    )
```

profile of v0, /device:TPU:8, one launch (start us, length us, event | category | flops | bytes accessed | tf_op | source)
XLA Modules:
  0.0 555.2 jit_solution(16775991105922428957)
XLA Ops:
  7.2 1.4 fusion.24
  10.4 81.0 %while.12 = (s32[]{:T(128)}, f32[32,8192]{1,0:T(8,128)S(1)}, bf16[32,4096]{1,0:T(8,128)(2,1)}, s32[]{:T(128)}, s32[]{:T(128)}, /*index=5*/s32[]{:T(128)}, s32[4]...) while((s32[]{:T(128)}, f32[32,8192]{1,0:T(8,128)S(1)}, ...), condition=%wide.region_1.2_spmd.clone, body=%wide.region_0.1_spmd.clone.sunk | while | flops 323494912 | bytes 2200785 | solution.py:39
  10.5 1.3 slice.29
  11.8 8.8 %convolution_add_fusion.2 = f32[32,8192]{1,0:T(8,128)S(1)} fusion(s32[]{:T(128)} %get-tuple-element.187, s32[]{:T(128)} %bitcast.6, s32[8192]{0:T(1024)S(1)} %iota_multiply_fusion.2, s32[512]{0:T(512)S(1)} %add_multiply_fusion.2, f32[32,8192]{1,0:T(8,128)S(1)} %get-tuple-element.169, pred[]{:T(512)S(6)} %compare.3, ...), kind=kOutput, calls=%fused_computation.8.clone.1 | convolution fusion | flops 323485696 | bytes 2165765 | tf_op jit(solution)/shard_map/while/body/dot_general | solution.py:37
  20.6 1.3 slice.29
  21.9 8.8 %convolution_add_fusion.2 = f32[32,8192]{1,0:T(8,128)S(1)} fusion(s32[]{:T(128)} %get-tuple-element.187, s32[]{:T(128)} %bitcast.6, s32[8192]{0:T(1024)S(1)} %iota_multiply_fusion.2, s32[512]{0:T(512)S(1)} %add_multiply_fusion.2, f32[32,8192]{1,0:T(8,128)S(1)} %get-tuple-element.169, pred[]{:T(512)S(6)} %compare.3, ...), kind=kOutput, calls=%fused_computation.8.clone.1 | convolution fusion | flops 323485696 | bytes 2165765 | tf_op jit(solution)/shard_map/while/body/dot_general | solution.py:37
  30.8 1.3 slice.29
  32.1 8.8 %convolution_add_fusion.2 = f32[32,8192]{1,0:T(8,128)S(1)} fusion(s32[]{:T(128)} %get-tuple-element.187, s32[]{:T(128)} %bitcast.6, s32[8192]{0:T(1024)S(1)} %iota_multiply_fusion.2, s32[512]{0:T(512)S(1)} %add_multiply_fusion.2, f32[32,8192]{1,0:T(8,128)S(1)} %get-tuple-element.169, pred[]{:T(512)S(6)} %compare.3, ...), kind=kOutput, calls=%fused_computation.8.clone.1 | convolution fusion | flops 323485696 | bytes 2165765 | tf_op jit(solution)/shard_map/while/body/dot_general | solution.py:37
  40.9 1.3 slice.29
  42.2 8.8 %convolution_add_fusion.2 = f32[32,8192]{1,0:T(8,128)S(1)} fusion(s32[]{:T(128)} %get-tuple-element.187, s32[]{:T(128)} %bitcast.6, s32[8192]{0:T(1024)S(1)} %iota_multiply_fusion.2, s32[512]{0:T(512)S(1)} %add_multiply_fusion.2, f32[32,8192]{1,0:T(8,128)S(1)} %get-tuple-element.169, pred[]{:T(512)S(6)} %compare.3, ...), kind=kOutput, calls=%fused_computation.8.clone.1 | convolution fusion | flops 323485696 | bytes 2165765 | tf_op jit(solution)/shard_map/while/body/dot_general | solution.py:37
  51.0 1.3 slice.29
  52.3 8.8 %convolution_add_fusion.2 = f32[32,8192]{1,0:T(8,128)S(1)} fusion(s32[]{:T(128)} %get-tuple-element.187, s32[]{:T(128)} %bitcast.6, s32[8192]{0:T(1024)S(1)} %iota_multiply_fusion.2, s32[512]{0:T(512)S(1)} %add_multiply_fusion.2, f32[32,8192]{1,0:T(8,128)S(1)} %get-tuple-element.169, pred[]{:T(512)S(6)} %compare.3, ...), kind=kOutput, calls=%fused_computation.8.clone.1 | convolution fusion | flops 323485696 | bytes 2165765 | tf_op jit(solution)/shard_map/while/body/dot_general | solution.py:37
  61.1 1.3 slice.29
  62.4 8.8 %convolution_add_fusion.2 = f32[32,8192]{1,0:T(8,128)S(1)} fusion(s32[]{:T(128)} %get-tuple-element.187, s32[]{:T(128)} %bitcast.6, s32[8192]{0:T(1024)S(1)} %iota_multiply_fusion.2, s32[512]{0:T(512)S(1)} %add_multiply_fusion.2, f32[32,8192]{1,0:T(8,128)S(1)} %get-tuple-element.169, pred[]{:T(512)S(6)} %compare.3, ...), kind=kOutput, calls=%fused_computation.8.clone.1 | convolution fusion | flops 323485696 | bytes 2165765 | tf_op jit(solution)/shard_map/while/body/dot_general | solution.py:37
  71.3 1.3 slice.29
  72.6 8.8 %convolution_add_fusion.2 = f32[32,8192]{1,0:T(8,128)S(1)} fusion(s32[]{:T(128)} %get-tuple-element.187, s32[]{:T(128)} %bitcast.6, s32[8192]{0:T(1024)S(1)} %iota_multiply_fusion.2, s32[512]{0:T(512)S(1)} %add_multiply_fusion.2, f32[32,8192]{1,0:T(8,128)S(1)} %get-tuple-element.169, pred[]{:T(512)S(6)} %compare.3, ...), kind=kOutput, calls=%fused_computation.8.clone.1 | convolution fusion | flops 323485696 | bytes 2165765 | tf_op jit(solution)/shard_map/while/body/dot_general | solution.py:37
  81.4 1.3 slice.29
  82.7 8.8 %convolution_add_fusion.2 = f32[32,8192]{1,0:T(8,128)S(1)} fusion(s32[]{:T(128)} %get-tuple-element.187, s32[]{:T(128)} %bitcast.6, s32[8192]{0:T(1024)S(1)} %iota_multiply_fusion.2, s32[512]{0:T(512)S(1)} %add_multiply_fusion.2, f32[32,8192]{1,0:T(8,128)S(1)} %get-tuple-element.169, pred[]{:T(512)S(6)} %compare.3, ...), kind=kOutput, calls=%fused_computation.8.clone.1 | convolution fusion | flops 323485696 | bytes 2165765 | tf_op jit(solution)/shard_map/while/body/dot_general | solution.py:37
  91.5 1.0 copy-done
  92.5 225.0 %reduce-scatter.2.cloned.1.call-done = f32[32,256]{1,0:T(8,128)} async-done(((f32[32,8192]{1,0:T(8,128)}), f32[32,256]{1,0:T(8,128)}) %reduce-scatter.2.cloned.1.call-update) | async-done | bytes 32784 | tf_op jit(solution)/shard_map/reduce_scatter | solution.py:45
  318.4 72.3 %psum.14 = f32[32]{0:T(128)S(1)} all-reduce(f32[32]{0:T(128)S(1)} %multiply_reduce_fusion), channel_id=1, replica_groups=mesh['param'=32,'ex'=16] {'param'}, use_global_device_ids=true, to_apply=%region_4.5 | all-reduce | flops 32 | bytes 256 | tf_op jit(solution)/shard_map/psum | solution.py:47
  391.5 17.1 %all_gather.3 = f32[512,256]{1,0:T(8,128)S(1)} all-gather(f32[32,256]{1,0:T(8,128)S(1)} %broadcast_multiply_fusion.1), channel_id=1, replica_groups=mesh['param'=32,'ex'=16] {'ex'}, dimensions={0}, use_global_device_ids=true | all-gather | bytes 557056 | tf_op jit(solution)/shard_map/all_gather | solution.py:49
  408.7 1.0 gather_fusion
  410.1 137.7 %psum.15 = f32[32,256]{1,0:T(8,128)S(1)} all-reduce(f32[32,256]{1,0:T(8,128)S(1)} %fusion.19), channel_id=1, replica_groups=mesh['param'=32,'ex'=16] {'param'}, use_global_device_ids=true, to_apply=%region_5.6 | all-reduce | flops 8192 | bytes 65536 | tf_op jit(solution)/shard_map/psum | solution.py:52
  (32 shorter events, 3.0 us)
Async XLA Ops:
  7.2 310.4 %reduce-scatter.2.cloned.1.call-start = ((), (), s32[]{:S(2)}) async-start(), calls=%async_computation.1 | async-start | bytes 1081344 | tf_op jit(solution)/shard_map/reduce_scatter | solution.py:45
  91.5 1.0 copy-start
  91.5 1.0 copy-start.2
  391.5 18.1 %copy-start.1 = (f32[32,256]{1,0:T(8,128)}, f32[32,256]{1,0:T(8,128)S(1)}, u32[]{:S(2)}) copy-start(f32[32,256]{1,0:T(8,128)S(1)} %broadcast_multiply_fusion.1) | copy-start | bytes 98308
Sparse Core Ops, SparseCore 0:
  92.6 224.9 reduce-scatter.1
where the time goes:
time: 556 us; the launch traced here: 555 us
  blocking collectives  227 us (41%)
  waiting for transfers between devices  225 us (40%)
  matrix products  70.5 us (13%)
  between operations  16 us (3%)
  local copies, waits for them, and re-layouts  13.7 us (2%)
    reduce_scatter x1, waiting for transfers between devices, local(): lax.psum_scatter(partial_sums, 'param', scatter_dimension=1, tiled=True)  225 us
    psum x1, blocking collectives, local(): scores = lax.psum(partial_dots, 'param') / scale_k  138 us
    psum x1, blocking collectives, local(): total_sq = lax.psum(own_squares, 'param')  72.3 us
    dot_general x8, matrix products, accumulate(): jnp.dot(gradient_slab, signs, preferred_element_type=jnp.float32)  70 us
    all_gather x1, blocking collectives, local(): pool_rows = lax.all_gather(features, 'ex', axis=0, tiled=True)  17.1 us
  transfers between devices with their start and end apart: 1, of which 1 were waited for; matrix products, arithmetic and copies ran while one was open for 0% of the time, Pallas kernels for 0%

commit v1 on v0

--- a/solution.py
+++ b/solution.py
@@ -1,10 +1,37 @@
+import functools
 import jax
 import jax.numpy as jnp
 from jax import lax
 from jax.sharding import PartitionSpec as P
+from jax.lax import axis_index, ppermute, psum
 
 K = 8192
 norm_eps = 1e-06
+
+
+def wait_skins(x_in, ax_name):
+    val2 = psum(1, axis_name=ax_name)
+    carry_out, out_arr, d_next = (val2, axis_index(ax_name), x_in.shape[0])
+    lanes = tuple(((d, (d + 1) % carry_out) for d in range(carry_out)))
+    pool = tuple(((d, (d - 1) % carry_out) for d in range(carry_out)))
+    b_now = jnp.zeros((*x_in.shape[:0], carry_out * d_next, *x_in.shape[1:]), x_in.dtype)
+    b_now = lax.dynamic_update_slice_in_dim(b_now, x_in, out_arr * d_next, axis=0)
+    piece_next = r1 = x_in
+    tmp = carry_out // 2
+    for s in range(1, tmp + 1):
+        piece_next = ppermute(piece_next, axis_name=ax_name, perm=lanes)
+        b_now = lax.dynamic_update_slice_in_dim(
+            b_now, piece_next, (out_arr - s) % carry_out * d_next, axis=0
+        )
+        if s < carry_out - tmp:
+            r1 = ppermute(r1, axis_name=ax_name, perm=pool)
+            b_now = lax.dynamic_update_slice_in_dim(
+                b_now, r1, (out_arr + s) % carry_out * d_next, axis=0
+            )
+    return b_now
+
+
+numbers_change = functools.partial(wait_skins, ax_name="ex")
 
 
 def sign_block(sign_hash_keys, first_row, row_count, col_count):
@@ -46,7 +73,7 @@
     own_squares = jnp.sum(projected * projected, axis=1)
     total_sq = lax.psum(own_squares, "param")
     features = projected * jnp.sqrt(scale_k / (total_sq + norm_eps))[:, None]
-    pool_rows = lax.all_gather(features, "ex", axis=0, tiled=True)
+    pool_rows = numbers_change(features)
     targets = jnp.take(pool_rows, target_indices, axis=0)
     partial_dots = jnp.dot(features, targets.T, precision=lax.Precision.HIGHEST)
     scores = lax.psum(partial_dots, "param") / scale_k

time: 556 us -> 575 us (1.034)
  the two profiles are of different devices: /device:TPU:8 before, /device:TPU:32 now
where the time goes in v1:
time: 575 us; the launch traced here: 574 us
  waiting for transfers between devices  240 us (42%)
  blocking collectives  210 us (37%)
  matrix products  70.3 us (12%)
  starting transfers between devices  20.7 us (4%)
  between operations  16 us (3%)
  local copies, waits for them, and re-layouts  13.8 us (2%)
    reduce_scatter x1, waiting for transfers between devices, local(): lax.psum_scatter(partial_sums, 'param', scatter_dimension=1, tiled=True)  225 us
    psum x1, blocking collectives, local(): scores = lax.psum(partial_dots, 'param') / scale_k  138 us
    psum x1, blocking collectives, local(): total_sq = lax.psum(own_squares, 'param')  72.2 us
    dot_general x8, matrix products, accumulate(): jnp.dot(gradient_slab, signs, preferred_element_type=jnp.float32)  69.9 us
    ppermute x7, starting transfers between devices, wait_skins(): r1 = ppermute(r1, axis_name=ax_name, perm=pool)  20.7 us
    ppermute x8, waiting for transfers between devices, wait_skins(): piece_next = ppermute(piece_next, axis_name=ax_name, perm=lanes)  15.6 us
  transfers between devices with their start and end apart: 16, of which 9 were waited for; matrix products, arithmetic and copies ran while one was open for 0% of the time, Pallas kernels for 0%

profile of v1, /device:TPU:32, one launch (start us, length us, event | category | flops | bytes accessed | tf_op | source)
XLA Modules:
  0.0 574.2 jit_solution(8599972284594733491)
XLA Ops:
  10.4 80.9 %while.12 = (s32[]{:T(128)}, f32[32,8192]{1,0:T(8,128)S(1)}, bf16[32,4096]{1,0:T(8,128)(2,1)}, s32[]{:T(128)}, s32[]{:T(128)}, /*index=5*/s32[]{:T(128)}, s32[4]...) while((s32[]{:T(128)}, f32[32,8192]{1,0:T(8,128)S(1)}, ...), condition=%wide.region_1.2_spmd.clone, body=%wide.region_0.1_spmd.clone.sunk | while | flops 323494912 | bytes 2200785 | solution.py:66
  11.8 8.7 %convolution_add_fusion.2 = f32[32,8192]{1,0:T(8,128)S(1)} fusion(s32[]{:T(128)} %get-tuple-element.189, s32[]{:T(128)} %bitcast.6, s32[8192]{0:T(1024)S(1)} %iota_multiply_fusion.2, s32[512]{0:T(512)S(1)} %add_multiply_fusion.2, f32[32,8192]{1,0:T(8,128)S(1)} %get-tuple-element.171, pred[]{:T(512)S(6)} %compare.18, ...), kind=kOutput, calls=%fused_computation.8.clone.1 | convolution fusion | flops 323485696 | bytes 2165765 | tf_op jit(solution)/shard_map/while/body/dot_general | solution.py:64
  21.9 8.7 %convolution_add_fusion.2 = f32[32,8192]{1,0:T(8,128)S(1)} fusion(s32[]{:T(128)} %get-tuple-element.189, s32[]{:T(128)} %bitcast.6, s32[8192]{0:T(1024)S(1)} %iota_multiply_fusion.2, s32[512]{0:T(512)S(1)} %add_multiply_fusion.2, f32[32,8192]{1,0:T(8,128)S(1)} %get-tuple-element.171, pred[]{:T(512)S(6)} %compare.18, ...), kind=kOutput, calls=%fused_computation.8.clone.1 | convolution fusion | flops 323485696 | bytes 2165765 | tf_op jit(solution)/shard_map/while/body/dot_general | solution.py:64
  32.0 8.7 %convolution_add_fusion.2 = f32[32,8192]{1,0:T(8,128)S(1)} fusion(s32[]{:T(128)} %get-tuple-element.189, s32[]{:T(128)} %bitcast.6, s32[8192]{0:T(1024)S(1)} %iota_multiply_fusion.2, s32[512]{0:T(512)S(1)} %add_multiply_fusion.2, f32[32,8192]{1,0:T(8,128)S(1)} %get-tuple-element.171, pred[]{:T(512)S(6)} %compare.18, ...), kind=kOutput, calls=%fused_computation.8.clone.1 | convolution fusion | flops 323485696 | bytes 2165765 | tf_op jit(solution)/shard_map/while/body/dot_general | solution.py:64
  42.1 8.7 %convolution_add_fusion.2 = f32[32,8192]{1,0:T(8,128)S(1)} fusion(s32[]{:T(128)} %get-tuple-element.189, s32[]{:T(128)} %bitcast.6, s32[8192]{0:T(1024)S(1)} %iota_multiply_fusion.2, s32[512]{0:T(512)S(1)} %add_multiply_fusion.2, f32[32,8192]{1,0:T(8,128)S(1)} %get-tuple-element.171, pred[]{:T(512)S(6)} %compare.18, ...), kind=kOutput, calls=%fused_computation.8.clone.1 | convolution fusion | flops 323485696 | bytes 2165765 | tf_op jit(solution)/shard_map/while/body/dot_general | solution.py:64
  52.2 8.7 %convolution_add_fusion.2 = f32[32,8192]{1,0:T(8,128)S(1)} fusion(s32[]{:T(128)} %get-tuple-element.189, s32[]{:T(128)} %bitcast.6, s32[8192]{0:T(1024)S(1)} %iota_multiply_fusion.2, s32[512]{0:T(512)S(1)} %add_multiply_fusion.2, f32[32,8192]{1,0:T(8,128)S(1)} %get-tuple-element.171, pred[]{:T(512)S(6)} %compare.18, ...), kind=kOutput, calls=%fused_computation.8.clone.1 | convolution fusion | flops 323485696 | bytes 2165765 | tf_op jit(solution)/shard_map/while/body/dot_general | solution.py:64
  62.3 8.7 %convolution_add_fusion.2 = f32[32,8192]{1,0:T(8,128)S(1)} fusion(s32[]{:T(128)} %get-tuple-element.189, s32[]{:T(128)} %bitcast.6, s32[8192]{0:T(1024)S(1)} %iota_multiply_fusion.2, s32[512]{0:T(512)S(1)} %add_multiply_fusion.2, f32[32,8192]{1,0:T(8,128)S(1)} %get-tuple-element.171, pred[]{:T(512)S(6)} %compare.18, ...), kind=kOutput, calls=%fused_computation.8.clone.1 | convolution fusion | flops 323485696 | bytes 2165765 | tf_op jit(solution)/shard_map/while/body/dot_general | solution.py:64
  72.5 8.7 %convolution_add_fusion.2 = f32[32,8192]{1,0:T(8,128)S(1)} fusion(s32[]{:T(128)} %get-tuple-element.189, s32[]{:T(128)} %bitcast.6, s32[8192]{0:T(1024)S(1)} %iota_multiply_fusion.2, s32[512]{0:T(512)S(1)} %add_multiply_fusion.2, f32[32,8192]{1,0:T(8,128)S(1)} %get-tuple-element.171, pred[]{:T(512)S(6)} %compare.18, ...), kind=kOutput, calls=%fused_computation.8.clone.1 | convolution fusion | flops 323485696 | bytes 2165765 | tf_op jit(solution)/shard_map/while/body/dot_general | solution.py:64
  82.6 8.7 %convolution_add_fusion.2 = f32[32,8192]{1,0:T(8,128)S(1)} fusion(s32[]{:T(128)} %get-tuple-element.189, s32[]{:T(128)} %bitcast.6, s32[8192]{0:T(1024)S(1)} %iota_multiply_fusion.2, s32[512]{0:T(512)S(1)} %add_multiply_fusion.2, f32[32,8192]{1,0:T(8,128)S(1)} %get-tuple-element.171, pred[]{:T(512)S(6)} %compare.18, ...), kind=kOutput, calls=%fused_computation.8.clone.1 | convolution fusion | flops 323485696 | bytes 2165765 | tf_op jit(solution)/shard_map/while/body/dot_general | solution.py:64
  92.4 224.8 %reduce-scatter.2.cloned.1.call-done = f32[32,256]{1,0:T(8,128)} async-done(((f32[32,8192]{1,0:T(8,128)}), f32[32,256]{1,0:T(8,128)}) %reduce-scatter.2.cloned.1.call-update) | async-done | bytes 32784 | tf_op jit(solution)/shard_map/reduce_scatter | solution.py:72
  318.1 72.2 %psum.14 = f32[32]{0:T(128)S(1)} all-reduce(f32[32]{0:T(128)S(1)} %multiply_reduce_fusion), channel_id=1, replica_groups=mesh['param'=32,'ex'=16] {'param'}, use_global_device_ids=true, to_apply=%region_4.5 | all-reduce | flops 32 | bytes 256 | tf_op jit(solution)/shard_map/psum | solution.py:74
  391.2 2.9 collective-permute-start.1
  394.2 1.6 collective-permute-done
  395.7 3.0 collective-permute-start.3
  398.7 1.6 collective-permute-done.2
  400.3 3.0 collective-permute-start.5
  404.9 3.0 collective-permute-start.7
  407.8 1.6 collective-permute-done.6
  409.4 3.0 collective-permute-start.9
  414.0 3.0 collective-permute-start.11
  418.5 3.0 collective-permute-start.13
  421.5 1.6 collective-permute-done.12
  423.1 4.5 collective-permute-done.14
  429.0 137.7 %psum.15 = f32[32,256]{1,0:T(8,128)S(1)} all-reduce(f32[32,256]{1,0:T(8,128)S(1)} %fusion.19), channel_id=1, replica_groups=mesh['param'=32,'ex'=16] {'param'}, use_global_device_ids=true, to_apply=%region_5.6 | all-reduce | flops 8192 | bytes 65536 | tf_op jit(solution)/shard_map/psum | solution.py:79
  (77 shorter events, 21.5 us)
Async XLA Ops:
  7.2 310.0 %reduce-scatter.2.cloned.1.call-start = ((), (), s32[]{:S(2)}) async-start(), calls=%async_computation.1 | async-start | bytes 1081344 | tf_op jit(solution)/shard_map/reduce_scatter | solution.py:72
  91.3 1.0 copy-start
  91.3 1.0 copy-start.2
  391.2 37.4 %copy-start.1 = (f32[32,256]{1,0:T(8,128)}, f32[32,256]{1,0:T(8,128)S(1)}, u32[]{:S(2)}) copy-start(f32[32,256]{1,0:T(8,128)S(1)} %get-tuple-element.105) | copy-start | bytes 98308
  391.2 4.6 collective-permute-start
  391.2 4.5 collective-permute-start.1
  395.7 4.6 collective-permute-start.2
  395.7 4.6 collective-permute-start.3
  400.3 4.6 collective-permute-start.4
  400.3 4.6 collective-permute-start.5
  404.8 4.6 collective-permute-start.6
  404.9 4.6 collective-permute-start.7
  409.4 4.6 collective-permute-start.8
  409.4 4.6 collective-permute-start.9
  413.9 4.6 collective-permute-start.10
  414.0 4.6 collective-permute-start.11
  418.5 4.6 collective-permute-start.12
  418.5 4.6 collective-permute-start.13
  423.0 4.6 collective-permute-start.14
Sparse Core Ops, SparseCore 0:
  92.4 224.7 reduce-scatter.1
